TPU v7x, 128 devices: a whole 4x4x4 slice. The times are simulated.
128 devices in a mesh: dp: 8 (over z, core), seq: 16 (over y, x).
Axes of the slice: x: 4, y: 4, z: 4, core: 2. Of those that a mesh axis runs over, the one named last changes fastest.
Arguments:
- tokens: bfloat16 [8, 8192, 2048], P('dp', 'seq'), may hold values from -6 to 6
- input_gain: bfloat16 [2048], replicated, may hold values from 0.099609375 to 1.8984375
- qkv_weight: bfloat16 [2048, 6144], P(None, ('dp', 'seq')), may hold values from -0.125 to 0.125
- head_gain: bfloat16 [2048], replicated, may hold values from 0.099609375 to 1.8984375
- prefix_state: float32 [8, 16, 128, 128], P('dp'), may hold values from -256 to 256
Outputs:
- attended: bfloat16 [8, 8192, 2048], P('dp', 'seq')
All inputs are finite; a program needn't handle non-finite values.
Results may differ from a plain program's by a relative error of at most 0.0061.
Values may be sent and summed in bfloat16 or wider, within the bound.
No kernel may reach another device: no remote copies, remote signals or barrier semaphores. Data moves between devices by JAX's collectives and lax.ppermute only.
A program may use at most 128 MiB of HBM per device.

v0:
```python
import jax
import jax.numpy as jnp
from jax import lax
from jax.sharding import PartitionSpec as P

D = 2048
H = 16
DH = 128
BLOCK = 512
epsilon = 1e-05


def feature_map(inputs):
    return jnp.where(inputs > 0, inputs + 1.0, jnp.exp(jnp.minimum(inputs, 0.0)))


def span_attention(queries, key_feats, values, memory, head_gain):
    num_blocks = queries.shape[0] // BLOCK
    causal = jnp.arange(BLOCK)[:, None] >= jnp.arange(BLOCK)[None, :]
    gains = head_gain.astype(jnp.float32).reshape(H, DH)

    def advance(running, blocks):
        query_blk, key_blk, value_blk = blocks
        carried = jnp.einsum(
            "bhd,hde->bhe",
            query_blk,
            running.astype(jnp.bfloat16),
            preferred_element_type=jnp.float32,
        )
        scores = jnp.einsum("bhd,chd->hbc", query_blk, key_blk, preferred_element_type=jnp.float32)
        scores = jnp.where(causal[None], scores, 0.0).astype(jnp.bfloat16)
        within = jnp.einsum("hbc,che->bhe", scores, value_blk, preferred_element_type=jnp.float32)
        numerator = carried + within
        scale = lax.rsqrt(jnp.mean(numerator * numerator, axis=-1, keepdims=True) + epsilon)
        running = running + jnp.einsum(
            "bhd,bhe->hde", key_blk, value_blk, preferred_element_type=jnp.float32
        )
        return (running, (numerator * scale * gains).astype(jnp.bfloat16))

    def shaped(inputs):
        return inputs.reshape(num_blocks, BLOCK, H, DH)

    final_memory, outputs = lax.scan(
        advance, memory, (shaped(queries), shaped(key_feats), shaped(values))
    )
    return outputs.reshape(num_blocks * BLOCK, H * DH)


def body(tokens, input_gain, qkv_weight, head_gain, prefix_state):
    inputs = tokens[0].astype(jnp.float32)
    normed = inputs * lax.rsqrt(jnp.mean(inputs * inputs, axis=-1, keepdims=True) + epsilon)
    normed = (normed * input_gain.astype(jnp.float32)).astype(jnp.bfloat16)
    tok_rows = normed.shape[0]
    projected = jnp.dot(
        normed,
        lax.all_gather(qkv_weight, ("dp", "seq"), axis=1, tiled=True),
        preferred_element_type=jnp.float32,
    )
    queries = feature_map(projected[:, :D]).astype(jnp.bfloat16).reshape(tok_rows, H, DH)
    key_feats = feature_map(projected[:, D : 2 * D]).astype(jnp.bfloat16).reshape(tok_rows, H, DH)
    values = projected[:, 2 * D :].astype(jnp.bfloat16).reshape(tok_rows, H, DH)
    local = jnp.einsum(
        "thd,the->hde", key_feats, values, preferred_element_type=jnp.float32
    ).astype(jnp.bfloat16)
    gathered = lax.all_gather(local[None], "seq", axis=0, tiled=True)
    my_index = lax.axis_index("seq")
    earlier = (jnp.arange(gathered.shape[0]) < my_index).astype(jnp.bfloat16)
    before = jnp.einsum("c,chde->hde", earlier, gathered, preferred_element_type=jnp.float32)
    memory = prefix_state[0] + before
    attended = span_attention(queries, key_feats, values, memory, head_gain)
    return attended[None]


def solution(mesh):
    placed = (P("dp", "seq", None), P(), P(None, ("dp", "seq")), P(), P("dp", None, None, None))
    return jax.shard_map(
        body, mesh=mesh, in_specs=placed, out_specs=P("dp", "seq", None), check_vma=False
    )
```

profile of v0, /device:TPU:1, one launch (start us, length us, event | category | flops | bytes accessed | tf_op | source)
XLA Modules:
  0.0 235.7 jit_solution(6228382882600847953)
XLA Ops:
  6.5 0.0 all-gather.4.cloned.1.call-start
  6.5 0.7 all-gather.4.cloned.1.call-update
  7.3 0.0 all-gather.6.cloned.1.call-start
  7.3 0.7 convert_element_type.38
  8.0 2.1 fusion.2
  10.1 97.0 %all-gather.4.cloned.1.call-done = bf16[2048,6144]{0,1:T(8,128)(2,1)} async-done(((bf16[2048,48]{0,1:T(8,128)(2,1)}), bf16[2048,6144]{0,1:T(8,128)(2,1)}) %all-gather.4.cloned.1.call-update) | async-done | bytes 25165840 | tf_op jit(solution)/shard_map/all_gather | solution.py:56
  107.1 20.0 %fusion.10 = f32[512,6144]{1,0:T(8,128)} fusion(bf16[2048,6144]{0,1:T(8,128)(2,1)} %all-gather.4.cloned.1.call-done, bf16[1,512,2048]{2,1,0:T(8,128)(2,1)} %param.5, f32[2048]{0:T(1024)S(1)} %convert_element_type.38, f32[512]{0:T(512)S(1)} %add_rsqrt_fusion.1), kind=kOutput, calls=%fused_computation.19 | convolution fusion | flops 12889096192 | bytes 39856128 | tf_op jit(solution)/shard_map/dot_general | solution.py:54
  127.1 5.7 %fusion.9 = (bf16[64,16,8,128]{3,2,1,0:T(8,128)(2,1)}, bf16[512,2048]{1,0:T(8,128)(2,1)}) fusion(f32[512,6144]{1,0:T(8,128)} %fusion.10), kind=kLoop, calls=%fused_computation.18 | loop fusion | flops 10485760 | bytes 12582912
  132.8 3.8 %slice.21 = bf16[512,2048]{1,0:T(8,128)(2,1)} slice(f32[512,6144]{1,0:T(8,128)} %fusion.10), slice={[0:512], [4096:6144]} | slice | bytes 4194304 | tf_op jit(solution)/shard_map/slice | solution.py:61
  136.6 2.9 %copy.22 = bf16[512,2048]{0,1:T(8,128)(2,1)S(1)} copy(bf16[512,2048]{1,0:T(8,128)(2,1)} %get-tuple-element.20) | data formatting | bytes 4194304 | tf_op jit(solution)/shard_map/reshape | solution.py:60
  139.5 0.0 copy-start.3
  139.5 4.0 %copy.23 = bf16[512,2048]{0,1:T(8,128)(2,1)} copy(bf16[512,2048]{1,0:T(8,128)(2,1)} %slice.21) | data formatting | bytes 4194304 | tf_op jit(solution)/shard_map/reshape | solution.py:61
  143.5 3.1 %convolution_convert_fusion = bf16[16,128,128]{2,1,0:T(8,128)(2,1)} fusion(bf16[512,16,128]{0,2,1:T(8,128)(2,1)S(1)} %bitcast.53, bf16[512,16,128]{0,2,1:T(8,128)(2,1)} %bitcast.55), kind=kOutput, calls=%fused_computation.27 | convolution fusion | flops 268697600 | bytes 4718592 | tf_op jit(solution)/shard_map/thd,the->hde/dot_general | solution.py:62
  146.6 0.0 all-gather.6.cloned.1.call-update
  146.6 0.1 iota_compare_fusion
  146.7 0.0 copy-done.3
  146.7 9.2 %fusion.8 = f32[16,128,512]{2,1,0:T(8,128)} fusion(bf16[512,16,128]{0,2,1:T(8,128)(2,1)} %bitcast.56, bf16[512,16,128]{0,2,1:T(8,128)(2,1)S(1)} %bitcast.54, pred[512,512]{1,0:T(8,128)(4,1)S(1)} %iota_compare_fusion, bf16[64,16,8,128]{3,2,1,0:T(8,128)(2,1)} %get-tuple-element.19), kind=kOutput, calls=%fused_computation.16 | convolution fusion | flops 2155872256 | bytes 10747904 | tf_op jit(solution)/shard_map/while/body/eval_jaxpr/hbc,che->bhe/dot_general | solution.py:32
  155.9 60.4 %all-gather.6.cloned.1.call-done = bf16[256,128,128]{2,1,0:T(8,128)(2,1)} async-done(((bf16[16,128,128]{2,1,0:T(8,128)(2,1)}), bf16[256,128,128]{2,1,0:T(8,128)(2,1)}) %all-gather.6.cloned.1.call-update) | async-done | bytes 8388624 | tf_op jit(solution)/shard_map/all_gather | solution.py:65
  216.3 0.0 copy-start
  216.3 0.0 copy-start.1
  216.3 0.0 copy-start.2
  216.3 8.4 %fusion = f32[1,16,128,128]{3,0,2,1:T(1,128)S(1)} fusion(bf16[16,16,128,128]{3,2,1,0:T(8,128)(2,1)} %bitcast.52, s32[]{:T(128)S(6)} %axis_index.12), kind=kOutput, calls=%fused_computation.1 | convolution fusion | flops 8388624 | bytes 9437188 | tf_op jit(solution)/shard_map/c,chde->hde/dot_general | solution.py:68
  224.8 0.0 copy-done
  224.8 0.0 copy-done.1
  224.8 0.0 copy-done.2
  224.8 1.0 fusion.5
  225.9 0.6 fusion.7
  226.5 2.4 %copy.17 = bf16[1,512,2048]{2,1,0:T(8,128)(2,1)} copy(bf16[1,512,2048]{1,2,0:T(8,128)(2,1)S(1)} %bitcast.57) | data formatting | bytes 4194304 | tf_op jit(solution)/shard_map/broadcast_in_dim;reshape | solution.py:71
  (3 shorter events, 0.0 us)
Async XLA Ops:
  6.5 100.6 %all-gather.4.cloned.1.call-start = ((), (), s32[]{:S(2)}) async-start(), calls=%async_computation | async-start | bytes 25362432 | tf_op jit(solution)/shard_map/all_gather | solution.py:56
  7.3 209.1 %all-gather.6.cloned.1.call-start = ((), (), s32[]{:S(2)}) async-start(), calls=%async_computation.1 | async-start | bytes 8912896 | tf_op jit(solution)/shard_map/all_gather | solution.py:65
  139.5 7.2 %copy-start.3 = (bf16[2048]{0:T(1024)(128)(2,1)S(1)}, bf16[2048]{0:T(1024)(128)(2,1)}, u32[]{:S(2)}) copy-start(bf16[2048]{0:T(1024)(128)(2,1)} %param.8) | copy-start | bytes 12292
  216.3 8.5 %copy-start = (bf16[64,16,8,128]{3,2,1,0:T(8,128)(2,1)S(1)}, bf16[64,16,8,128]{3,2,1,0:T(8,128)(2,1)}, u32[]{:S(2)}) copy-start(bf16[64,16,8,128]{3,2,1,0:T(8,128)(2,1)} %get-tuple-element.19) | copy-start | bytes 6291460
  216.3 8.5 %copy-start.1 = (f32[16,128,512]{2,1,0:T(8,128)S(1)}, f32[16,128,512]{2,1,0:T(8,128)}, u32[]{:S(2)}) copy-start(f32[16,128,512]{2,1,0:T(8,128)} %fusion.8) | copy-start | bytes 12582916
  216.3 8.5 %copy-start.2 = (f32[1,16,128,128]{3,2,1,0:T(8,128)S(1)}, f32[1,16,128,128]{3,2,1,0:T(8,128)}, u32[]{:S(2)}) copy-start(f32[1,16,128,128]{3,2,1,0:T(8,128)} %param.9) | copy-start | bytes 3145732
Sparse Core Ops, SparseCore 0:
  10.4 96.6 all-gather.3
  146.7 69.5 all-gather.5
where the time goes:
time: 236 us
  waiting for transfers between devices  158 us (67%)
  matrix products  41.8 us (18%)
  between operations  13.5 us (6%)
  local copies, waits for them, and re-layouts  13 us (6%)
  other arithmetic  9.23 us (4%)
    all_gather x1, waiting for transfers between devices, body(): lax.all_gather(qkv_weight, ('dp', 'seq'), axis=1, tiled=True)  97 us
    all_gather x1, waiting for transfers between devices, body(): gathered = lax.all_gather(local[None], 'seq', axis=0, tiled=True)  60.4 us
    dot_general x1, matrix products, body(): jnp.dot(normed, lax.all_gather(qkv_weight, ('dp', 'seq'), axis=1, tiled=T...  20 us
    dot_general x1, matrix products, advance(): jnp.einsum('hbc,che->bhe', scores, value_blk, preferred_element_type=jnp....  9.24 us
    dot_general x1, matrix products, body(): jnp.einsum('c,chde->hde', earlier, gathered, preferred_element_type=jnp.f...  8.45 us
    unnamed x1, other arithmetic  5.73 us
  transfers between devices with their start and end apart: 2, of which 2 were waited for; matrix products, arithmetic and copies ran while one was open for 5% of the time, Pallas kernels for 0%

commit v1 on v0

--- a/solution.py
+++ b/solution.py
@@ -62,7 +62,16 @@
     local = jnp.einsum(
         "thd,the->hde", key_feats, values, preferred_element_type=jnp.float32
     ).astype(jnp.bfloat16)
-    gathered = lax.all_gather(local[None], "seq", axis=0, tiled=True)
+    ways = lax.axis_size("seq")
+    up = [(d, (d + 1) % ways) for d in range(ways)]
+    down = [(d, (d - 1) % ways) for d in range(ways)]
+    earlier_2, later = ([local[None]], [local[None]])
+    for _ in range(ways // 2):
+        earlier_2.append(lax.ppermute(earlier_2[-1], "seq", up))
+    for _ in range((ways - 1) // 2):
+        later.append(lax.ppermute(later[-1], "seq", down))
+    line = jnp.concatenate([*earlier_2[::-1], *later[1:]], axis=0)
+    gathered = jnp.roll(line, (lax.axis_index("seq") - ways // 2) * local[None].shape[0], axis=0)
     my_index = lax.axis_index("seq")
     earlier = (jnp.arange(gathered.shape[0]) < my_index).astype(jnp.bfloat16)
     before = jnp.einsum("c,chde->hde", earlier, gathered, preferred_element_type=jnp.float32)

time: 236 us -> 343 us (1.45)
  the two profiles are of different devices: /device:TPU:1 before, /device:TPU:0 now
where the time goes in v1:
time: 343 us; the launch traced here: 341 us
  waiting for transfers between devices  165 us (48%)
  local copies, waits for them, and re-layouts  71.3 us (21%)
  matrix products  42.2 us (12%)
  starting transfers between devices  39.8 us (12%)
  between operations  13.6 us (4%)
  other arithmetic  9.21 us (3%)
    all_gather x1, waiting for transfers between devices, body(): lax.all_gather(qkv_weight, ('dp', 'seq'), axis=1, tiled=True)  95.9 us
    ppermute x8, waiting for transfers between devices, body(): earlier_2.append(lax.ppermute(earlier_2[-1], 'seq', up))  68.8 us
    unnamed x65, local copies, waits for them, and re-layouts  47.1 us
    ppermute x7, starting transfers between devices, body(): later.append(lax.ppermute(later[-1], 'seq', down))  38.2 us
    dot_general x1, matrix products, body(): jnp.dot(normed, lax.all_gather(qkv_weight, ('dp', 'seq'), axis=1, tiled=T...  20 us
    dynamic_slice x1, local copies, waits for them, and re-layouts, body(): jnp.roll(line, (lax.axis_index('seq') - ways // 2) * local[None].shape[0]...  10.4 us
    dot_general x1, matrix products, advance(): jnp.einsum('hbc,che->bhe', scores, value_blk, preferred_element_type=jnp....  9.23 us
    dot_general x1, matrix products, body(): jnp.einsum('c,chde->hde', earlier, gathered, preferred_element_type=jnp.f...  8.3 us
  transfers between devices with their start and end apart: 16, of which 8 were waited for; matrix products, arithmetic and copies ran while one was open for 11% of the time, Pallas kernels for 0%

profile of v1, /device:TPU:0, one launch (start us, length us, event | category | flops | bytes accessed | tf_op | source)
XLA Modules:
  0.0 341.5 jit_solution(11107455600406593159)
XLA Ops:
  7.9 2.1 fusion.2
  10.0 95.9 %all-gather.2.cloned.1.call-done = bf16[2048,6144]{0,1:T(8,128)(2,1)} async-done(((bf16[2048,48]{0,1:T(8,128)(2,1)}), bf16[2048,6144]{0,1:T(8,128)(2,1)}) %all-gather.2.cloned.1.call-update) | async-done | bytes 25165840 | tf_op jit(solution)/shard_map/all_gather | solution.py:56
  105.9 20.0 %fusion.10 = f32[512,6144]{1,0:T(8,128)} fusion(bf16[2048,6144]{0,1:T(8,128)(2,1)} %all-gather.2.cloned.1.call-done, bf16[1,512,2048]{2,1,0:T(8,128)(2,1)} %param.5, f32[2048]{0:T(1024)S(1)} %convert_element_type.38, f32[512]{0:T(512)S(1)} %add_rsqrt_fusion.1), kind=kOutput, calls=%fused_computation.19 | convolution fusion | flops 12889096192 | bytes 39856128 | tf_op jit(solution)/shard_map/dot_general | solution.py:54
  126.0 3.8 %slice.21 = bf16[512,2048]{1,0:T(8,128)(2,1)} slice(f32[512,6144]{1,0:T(8,128)} %fusion.10), slice={[0:512], [4096:6144]} | slice | bytes 4194304 | tf_op jit(solution)/shard_map/slice | solution.py:61
  129.8 5.7 %fusion.9 = (bf16[64,16,8,128]{3,2,1,0:T(8,128)(2,1)}, bf16[512,2048]{1,0:T(8,128)(2,1)}) fusion(f32[512,6144]{1,0:T(8,128)} %fusion.10), kind=kLoop, calls=%fused_computation.18 | loop fusion | flops 10485760 | bytes 12582912
  135.5 2.9 copy.17
  138.4 3.9 %copy.16 = bf16[512,2048]{0,1:T(8,128)(2,1)} copy(bf16[512,2048]{1,0:T(8,128)(2,1)} %get-tuple-element.20) | data formatting | bytes 4194304 | tf_op jit(solution)/shard_map/reshape | solution.py:60
  142.3 2.3 fusion.21
  144.6 1.5 collective-permute-start
  146.1 15.9 %collective-permute-done = bf16[1,16,128,128]{3,2,1,0:T(8,128)(2,1)S(1)} collective-permute-done((bf16[1,16,128,128]{3,2,1,0:T(8,128)(2,1)S(1)}, bf16[1,16,128,128]{3,2,1,0:T(8,128)(2,1)S(1)}, u32[]{:S(2)}, u32[]{:S(2)}) %collective-permute-start) | collective-permute-done | bytes 524320 | tf_op jit(solution)/shard_map/ppermute | solution.py:70
  162.1 5.3 %collective-permute-start.8 = (bf16[1,16,128,128]{3,2,1,0:T(8,128)(2,1)S(1)}, bf16[1,16,128,128]{3,2,1,0:T(8,128)(2,1)S(1)}, u32[]{:S(2)}, u32[]{:S(2)}) collective-permute-start(bf16[1,16,128,128]{3,2,1,0:T(8,128)(2,1)S(1)} %fusion.21), channel_id=1, source_target_pairs={{0,15},{1,0},{2,1},{3,2},{4,3},{5,4},{6,5},{7,6},{8,7},{9,8},{10,9... | collective-permute-start | bytes 1572872 | tf_op jit(solution)/shard_map/ppermute | solution.py:72
  167.4 11.2 %collective-permute-done.1 = bf16[1,16,128,128]{3,2,1,0:T(8,128)(2,1)S(1)} collective-permute-done((bf16[1,16,128,128]{3,2,1,0:T(8,128)(2,1)S(1)}, bf16[1,16,128,128]{3,2,1,0:T(8,128)(2,1)S(1)}, u32[]{:S(2)}, u32[]{:S(2)}) %collective-permute-start.1) | collective-permute-done | bytes 524320 | tf_op jit(solution)/shard_map/ppermute | solution.py:70
  179.5 5.3 %collective-permute-start.9 = (bf16[1,16,128,128]{3,2,1,0:T(8,128)(2,1)S(1)}, bf16[1,16,128,128]{3,2,1,0:T(8,128)(2,1)S(1)}, u32[]{:S(2)}, u32[]{:S(2)}) collective-permute-start(bf16[1,16,128,128]{3,2,1,0:T(8,128)(2,1)S(1)} %collective-permute-done.8), channel_id=1, source_target_pairs={{0,15},{1,0},{2,1},{3,2},{4,3},{5,4},{6,5},{7,6},{8,7},{9,8},{10,9... | collective-permute-start | bytes 1572872 | tf_op jit(solution)/shard_map/ppermute | solution.py:72
  184.8 9.5 %collective-permute-done.2 = bf16[1,16,128,128]{3,2,1,0:T(8,128)(2,1)S(1)} collective-permute-done((bf16[1,16,128,128]{3,2,1,0:T(8,128)(2,1)S(1)}, bf16[1,16,128,128]{3,2,1,0:T(8,128)(2,1)S(1)}, u32[]{:S(2)}, u32[]{:S(2)}) %collective-permute-start.2) | collective-permute-done | bytes 524320 | tf_op jit(solution)/shard_map/ppermute | solution.py:70
  194.4 5.8 %collective-permute-start.10 = (bf16[1,16,128,128]{3,2,1,0:T(8,128)(2,1)S(1)}, bf16[1,16,128,128]{3,2,1,0:T(8,128)(2,1)S(1)}, u32[]{:S(2)}, u32[]{:S(2)}) collective-permute-start(bf16[1,16,128,128]{3,2,1,0:T(8,128)(2,1)S(1)} %collective-permute-done.9), channel_id=1, source_target_pairs={{0,15},{1,0},{2,1},{3,2},{4,3},{5,4},{6,5},{7,6},{8,7},{9,8},{10,9... | collective-permute-start | bytes 1572872 | tf_op jit(solution)/shard_map/ppermute | solution.py:72
  200.2 8.9 %collective-permute-done.3 = bf16[1,16,128,128]{3,2,1,0:T(8,128)(2,1)S(1)} collective-permute-done((bf16[1,16,128,128]{3,2,1,0:T(8,128)(2,1)S(1)}, bf16[1,16,128,128]{3,2,1,0:T(8,128)(2,1)S(1)}, u32[]{:S(2)}, u32[]{:S(2)}) %collective-permute-start.3) | collective-permute-done | bytes 524320 | tf_op jit(solution)/shard_map/ppermute | solution.py:70
  209.1 5.6 %collective-permute-start.11 = (bf16[1,16,128,128]{3,2,1,0:T(8,128)(2,1)S(1)}, bf16[1,16,128,128]{3,2,1,0:T(8,128)(2,1)}, u32[]{:S(2)}, u32[]{:S(2)}) collective-permute-start(bf16[1,16,128,128]{3,2,1,0:T(8,128)(2,1)S(1)} %collective-permute-done.10), channel_id=1, source_target_pairs={{0,15},{1,0},{2,1},{3,2},{4,3},{5,4},{6,5},{7,6},{8,7},{9,8},{10,9... | collective-permute-start | bytes 1572872 | tf_op jit(solution)/shard_map/ppermute | solution.py:72
  214.7 8.2 %collective-permute-done.4 = bf16[1,16,128,128]{3,2,1,0:T(8,128)(2,1)S(1)} collective-permute-done((bf16[1,16,128,128]{3,2,1,0:T(8,128)(2,1)S(1)}, bf16[1,16,128,128]{3,2,1,0:T(8,128)(2,1)S(1)}, u32[]{:S(2)}, u32[]{:S(2)}) %collective-permute-start.4) | collective-permute-done | bytes 524320 | tf_op jit(solution)/shard_map/ppermute | solution.py:70
  223.0 5.4 %collective-permute-start.12 = (bf16[1,16,128,128]{3,2,1,0:T(8,128)(2,1)}, bf16[1,16,128,128]{3,2,1,0:T(8,128)(2,1)}, u32[]{:S(2)}, u32[]{:S(2)}) collective-permute-start(bf16[1,16,128,128]{3,2,1,0:T(8,128)(2,1)} %collective-permute-done.11), channel_id=1, source_target_pairs={{0,15},{1,0},{2,1},{3,2},{4,3},{5,4},{6,5},{7,6},{8,7},{9,8},{10,9... | collective-permute-start | bytes 1572872 | tf_op jit(solution)/shard_map/ppermute | solution.py:72
  228.3 7.6 %collective-permute-done.5 = bf16[1,16,128,128]{3,2,1,0:T(8,128)(2,1)} collective-permute-done((bf16[1,16,128,128]{3,2,1,0:T(8,128)(2,1)S(1)}, bf16[1,16,128,128]{3,2,1,0:T(8,128)(2,1)}, u32[]{:S(2)}, u32[]{:S(2)}) %collective-permute-start.5) | collective-permute-done | bytes 524320 | tf_op jit(solution)/shard_map/ppermute | solution.py:70
  236.1 5.4 %collective-permute-start.13 = (bf16[1,16,128,128]{3,2,1,0:T(8,128)(2,1)}, bf16[1,16,128,128]{3,2,1,0:T(8,128)(2,1)}, u32[]{:S(2)}, u32[]{:S(2)}) collective-permute-start(bf16[1,16,128,128]{3,2,1,0:T(8,128)(2,1)} %collective-permute-done.12), channel_id=1, source_target_pairs={{0,15},{1,0},{2,1},{3,2},{4,3},{5,4},{6,5},{7,6},{8,7},{9,8},{10,9... | collective-permute-start | bytes 1572872 | tf_op jit(solution)/shard_map/ppermute | solution.py:72
  241.5 7.3 %collective-permute-done.6 = bf16[1,16,128,128]{3,2,1,0:T(8,128)(2,1)} collective-permute-done((bf16[1,16,128,128]{3,2,1,0:T(8,128)(2,1)}, bf16[1,16,128,128]{3,2,1,0:T(8,128)(2,1)}, u32[]{:S(2)}, u32[]{:S(2)}) %collective-permute-start.6) | collective-permute-done | bytes 524320 | tf_op jit(solution)/shard_map/ppermute | solution.py:70
  248.8 9.2 %fusion.8 = f32[16,128,512]{2,1,0:T(8,128)} fusion(bf16[512,16,128]{0,2,1:T(8,128)(2,1)S(1)} %bitcast.54, bf16[512,16,128]{0,2,1:T(8,128)(2,1)} %bitcast.56, pred[512,512]{1,0:T(8,128)(4,1)S(1)} %iota_compare_fusion, bf16[64,16,8,128]{3,2,1,0:T(8,128)(2,1)} %get-tuple-element.19), kind=kOutput, calls=%fused_computation.16 | convolution fusion | flops 2155872256 | bytes 10747904 | tf_op jit(solution)/shard_map/while/body/eval_jaxpr/hbc,che->bhe/dot_general | solution.py:32
  258.1 5.4 %collective-permute-start.14 = (bf16[1,16,128,128]{3,2,1,0:T(8,128)(2,1)}, bf16[1,16,128,128]{3,2,1,0:T(8,128)(2,1)S(1)}, u32[]{:S(2)}, u32[]{:S(2)}) collective-permute-start(bf16[1,16,128,128]{3,2,1,0:T(8,128)(2,1)} %collective-permute-done.13), channel_id=1, source_target_pairs={{0,15},{1,0},{2,1},{3,2},{4,3},{5,4},{6,5},{7,6},{8,7},{9,8},{10,9... | collective-permute-start | bytes 1572872 | tf_op jit(solution)/shard_map/ppermute | solution.py:72
  263.5 1.9 constant_dynamic-update-slice_fusion.31
  265.4 1.9 constant_dynamic-update-slice_fusion.30
  267.3 1.9 constant_dynamic-update-slice_fusion.29
  269.2 1.9 constant_dynamic-update-slice_fusion.28
  271.1 1.9 constant_dynamic-update-slice_fusion.27
  273.0 1.9 constant_dynamic-update-slice_fusion.26
  274.9 1.9 constant_dynamic-update-slice_fusion.25
  278.4 1.9 constant_dynamic-update-slice_fusion.22
  280.3 1.9 constant_dynamic-update-slice_fusion.21
  282.2 1.9 constant_dynamic-update-slice_fusion.20
  284.1 1.9 constant_dynamic-update-slice_fusion.19
  286.1 1.9 constant_dynamic-update-slice_fusion.18
  287.9 1.9 constant_dynamic-update-slice_fusion.17
  289.8 0.9 constant_dynamic-update-slice_fusion.16
  290.7 2.0 constant_dynamic-update-slice_fusion.15
  292.7 1.9 constant_dynamic-update-slice_fusion.14
  294.6 1.9 constant_dynamic-update-slice_fusion.13
  304.1 1.9 constant_dynamic-update-slice_fusion.3
  306.0 1.9 constant_dynamic-update-slice_fusion.2
  307.9 1.9 constant_dynamic-update-slice_fusion.1
  310.6 10.4 %constant_dynamic-slice_fusion = bf16[16,16,128,128]{3,2,1,0:T(8,128)(2,1)} fusion(bf16[32,16,128,128]{3,2,1,0:T(8,128)(2,1)} %constant_dynamic-update-slice_fusion, s32[]{:T(128)S(6)} %select_n.27), kind=kLoop, calls=%fused_computation.70 | loop fusion | bytes 16777220 | tf_op jit(solution)/shard_map/jit(_roll_dynamic)/dynamic_slice | solution.py:74
  321.0 8.3 %fusion = f32[1,16,128,128]{3,0,2,1:T(1,128)S(1)} fusion(bf16[16,16,128,128]{3,2,1,0:T(8,128)(2,1)} %constant_dynamic-slice_fusion, s32[]{:T(128)S(6)} %axis_index.16), kind=kOutput, calls=%fused_computation.1 | convolution fusion | flops 8388624 | bytes 9437188 | tf_op jit(solution)/shard_map/c,chde->hde/dot_general | solution.py:77
  329.3 2.3 fusion.5
  332.3 2.4 copy.11
  (69 shorter events, 13.2 us)
Async XLA Ops:
  6.5 99.4 %all-gather.2.cloned.1.call-start = ((), (), s32[]{:S(2)}) async-start(), calls=%async_computation | async-start | bytes 25362432 | tf_op jit(solution)/shard_map/all_gather | solution.py:56
  126.0 110.1 %copy-start.16 = (bf16[2048]{0:T(1024)(128)(2,1)S(1)}, bf16[2048]{0:T(1024)(128)(2,1)}, u32[]{:S(2)}) copy-start(bf16[2048]{0:T(1024)(128)(2,1)} %param.8) | copy-start | bytes 12292
  144.6 17.5 %collective-permute-start = (bf16[1,16,128,128]{3,2,1,0:T(8,128)(2,1)S(1)}, bf16[1,16,128,128]{3,2,1,0:T(8,128)(2,1)S(1)}, u32[]{:S(2)}, u32[]{:S(2)}) collective-permute-start(bf16[1,16,128,128]{3,2,1,0:T(8,128)(2,1)S(1)} %fusion.21), channel_id=1, source_target_pairs={{0,1},{1,2},{2,3},{3,4},{4,5},{5,6},{6,7},{7,8},{8,9},{9,10},{10,1... | collective-permute-start | bytes 1572872 | tf_op jit(solution)/shard_map/ppermute | solution.py:70
  162.1 16.6 %collective-permute-start.1 = (bf16[1,16,128,128]{3,2,1,0:T(8,128)(2,1)S(1)}, bf16[1,16,128,128]{3,2,1,0:T(8,128)(2,1)S(1)}, u32[]{:S(2)}, u32[]{:S(2)}) collective-permute-start(bf16[1,16,128,128]{3,2,1,0:T(8,128)(2,1)S(1)} %collective-permute-done), channel_id=1, source_target_pairs={{0,1},{1,2},{2,3},{3,4},{4,5},{5,6},{6,7},{7,8},{8,9},{9,10},{10,1... | collective-permute-start | bytes 1572872 | tf_op jit(solution)/shard_map/ppermute | solution.py:70
  162.1 16.6 %collective-permute-start.8 = (bf16[1,16,128,128]{3,2,1,0:T(8,128)(2,1)S(1)}, bf16[1,16,128,128]{3,2,1,0:T(8,128)(2,1)S(1)}, u32[]{:S(2)}, u32[]{:S(2)}) collective-permute-start(bf16[1,16,128,128]{3,2,1,0:T(8,128)(2,1)S(1)} %fusion.21), channel_id=1, source_target_pairs={{0,15},{1,0},{2,1},{3,2},{4,3},{5,4},{6,5},{7,6},{8,7},{9,8},{10,9... | collective-permute-start | bytes 1572872 | tf_op jit(solution)/shard_map/ppermute | solution.py:72
  178.7 15.7 %copy-start.4 = (bf16[1,16,128,128]{3,2,1,0:T(8,128)(2,1)}, bf16[1,16,128,128]{3,2,1,0:T(8,128)(2,1)S(1)}, u32[]{:S(2)}) copy-start(bf16[1,16,128,128]{3,2,1,0:T(8,128)(2,1)S(1)} %collective-permute-done.1) | copy-start | bytes 1572868
  178.7 15.7 %collective-permute-start.2 = (bf16[1,16,128,128]{3,2,1,0:T(8,128)(2,1)S(1)}, bf16[1,16,128,128]{3,2,1,0:T(8,128)(2,1)S(1)}, u32[]{:S(2)}, u32[]{:S(2)}) collective-permute-start(bf16[1,16,128,128]{3,2,1,0:T(8,128)(2,1)S(1)} %collective-permute-done.1), channel_id=1, source_target_pairs={{0,1},{1,2},{2,3},{3,4},{4,5},{5,6},{6,7},{7,8},{8,9},{9,10},{10,1... | collective-permute-start | bytes 1572872 | tf_op jit(solution)/shard_map/ppermute | solution.py:70
  178.7 0.8 copy-start.2
  179.5 14.9 %collective-permute-start.9 = (bf16[1,16,128,128]{3,2,1,0:T(8,128)(2,1)S(1)}, bf16[1,16,128,128]{3,2,1,0:T(8,128)(2,1)S(1)}, u32[]{:S(2)}, u32[]{:S(2)}) collective-permute-start(bf16[1,16,128,128]{3,2,1,0:T(8,128)(2,1)S(1)} %collective-permute-done.8), channel_id=1, source_target_pairs={{0,15},{1,0},{2,1},{3,2},{4,3},{5,4},{6,5},{7,6},{8,7},{9,8},{10,9... | collective-permute-start | bytes 1572872 | tf_op jit(solution)/shard_map/ppermute | solution.py:72
  194.3 14.8 %copy-start.8 = (bf16[1,16,128,128]{3,2,1,0:T(8,128)(2,1)}, bf16[1,16,128,128]{3,2,1,0:T(8,128)(2,1)S(1)}, u32[]{:S(2)}) copy-start(bf16[1,16,128,128]{3,2,1,0:T(8,128)(2,1)S(1)} %collective-permute-done.2) | copy-start | bytes 1572868
  194.3 14.8 %collective-permute-start.3 = (bf16[1,16,128,128]{3,2,1,0:T(8,128)(2,1)S(1)}, bf16[1,16,128,128]{3,2,1,0:T(8,128)(2,1)S(1)}, u32[]{:S(2)}, u32[]{:S(2)}) collective-permute-start(bf16[1,16,128,128]{3,2,1,0:T(8,128)(2,1)S(1)} %collective-permute-done.2), channel_id=1, source_target_pairs={{0,1},{1,2},{2,3},{3,4},{4,5},{5,6},{6,7},{7,8},{8,9},{9,10},{10,1... | collective-permute-start | bytes 1572872 | tf_op jit(solution)/shard_map/ppermute | solution.py:70
  194.4 5.8 %copy-start.6 = (bf16[1,16,128,128]{3,2,1,0:T(8,128)(2,1)}, bf16[1,16,128,128]{3,2,1,0:T(8,128)(2,1)S(1)}, u32[]{:S(2)}) copy-start(bf16[1,16,128,128]{3,2,1,0:T(8,128)(2,1)S(1)} %collective-permute-done.9) | copy-start | bytes 1572868
  194.4 14.7 %collective-permute-start.10 = (bf16[1,16,128,128]{3,2,1,0:T(8,128)(2,1)S(1)}, bf16[1,16,128,128]{3,2,1,0:T(8,128)(2,1)S(1)}, u32[]{:S(2)}, u32[]{:S(2)}) collective-permute-start(bf16[1,16,128,128]{3,2,1,0:T(8,128)(2,1)S(1)} %collective-permute-done.9), channel_id=1, source_target_pairs={{0,15},{1,0},{2,1},{3,2},{4,3},{5,4},{6,5},{7,6},{8,7},{9,8},{10,9... | collective-permute-start | bytes 1572872 | tf_op jit(solution)/shard_map/ppermute | solution.py:72
  209.1 13.8 %copy-start.12 = (bf16[1,16,128,128]{3,2,1,0:T(8,128)(2,1)}, bf16[1,16,128,128]{3,2,1,0:T(8,128)(2,1)S(1)}, u32[]{:S(2)}) copy-start(bf16[1,16,128,128]{3,2,1,0:T(8,128)(2,1)S(1)} %collective-permute-done.3) | copy-start | bytes 1572868
  209.1 13.8 %collective-permute-start.4 = (bf16[1,16,128,128]{3,2,1,0:T(8,128)(2,1)S(1)}, bf16[1,16,128,128]{3,2,1,0:T(8,128)(2,1)S(1)}, u32[]{:S(2)}, u32[]{:S(2)}) collective-permute-start(bf16[1,16,128,128]{3,2,1,0:T(8,128)(2,1)S(1)} %collective-permute-done.3), channel_id=1, source_target_pairs={{0,1},{1,2},{2,3},{3,4},{4,5},{5,6},{6,7},{7,8},{8,9},{9,10},{10,1... | collective-permute-start | bytes 1572872 | tf_op jit(solution)/shard_map/ppermute | solution.py:70
  209.1 5.6 %copy-start.10 = (bf16[1,16,128,128]{3,2,1,0:T(8,128)(2,1)}, bf16[1,16,128,128]{3,2,1,0:T(8,128)(2,1)S(1)}, u32[]{:S(2)}) copy-start(bf16[1,16,128,128]{3,2,1,0:T(8,128)(2,1)S(1)} %collective-permute-done.10) | copy-start | bytes 1572868
  209.1 13.8 %collective-permute-start.11 = (bf16[1,16,128,128]{3,2,1,0:T(8,128)(2,1)S(1)}, bf16[1,16,128,128]{3,2,1,0:T(8,128)(2,1)}, u32[]{:S(2)}, u32[]{:S(2)}) collective-permute-start(bf16[1,16,128,128]{3,2,1,0:T(8,128)(2,1)S(1)} %collective-permute-done.10), channel_id=1, source_target_pairs={{0,15},{1,0},{2,1},{3,2},{4,3},{5,4},{6,5},{7,6},{8,7},{9,8},{10,9... | collective-permute-start | bytes 1572872 | tf_op jit(solution)/shard_map/ppermute | solution.py:72
  222.9 5.4 %copy-start.14 = (bf16[1,16,128,128]{3,2,1,0:T(8,128)(2,1)}, bf16[1,16,128,128]{3,2,1,0:T(8,128)(2,1)S(1)}, u32[]{:S(2)}) copy-start(bf16[1,16,128,128]{3,2,1,0:T(8,128)(2,1)S(1)} %collective-permute-done.4) | copy-start | bytes 1572868
  222.9 13.0 %collective-permute-start.5 = (bf16[1,16,128,128]{3,2,1,0:T(8,128)(2,1)S(1)}, bf16[1,16,128,128]{3,2,1,0:T(8,128)(2,1)}, u32[]{:S(2)}, u32[]{:S(2)}) collective-permute-start(bf16[1,16,128,128]{3,2,1,0:T(8,128)(2,1)S(1)} %collective-permute-done.4), channel_id=1, source_target_pairs={{0,1},{1,2},{2,3},{3,4},{4,5},{5,6},{6,7},{7,8},{8,9},{9,10},{10,1... | collective-permute-start | bytes 1572872 | tf_op jit(solution)/shard_map/ppermute | solution.py:70
  223.0 13.1 %collective-permute-start.12 = (bf16[1,16,128,128]{3,2,1,0:T(8,128)(2,1)}, bf16[1,16,128,128]{3,2,1,0:T(8,128)(2,1)}, u32[]{:S(2)}, u32[]{:S(2)}) collective-permute-start(bf16[1,16,128,128]{3,2,1,0:T(8,128)(2,1)} %collective-permute-done.11), channel_id=1, source_target_pairs={{0,15},{1,0},{2,1},{3,2},{4,3},{5,4},{6,5},{7,6},{8,7},{9,8},{10,9... | collective-permute-start | bytes 1572872 | tf_op jit(solution)/shard_map/ppermute | solution.py:72
  236.0 12.8 %collective-permute-start.6 = (bf16[1,16,128,128]{3,2,1,0:T(8,128)(2,1)}, bf16[1,16,128,128]{3,2,1,0:T(8,128)(2,1)}, u32[]{:S(2)}, u32[]{:S(2)}) collective-permute-start(bf16[1,16,128,128]{3,2,1,0:T(8,128)(2,1)} %collective-permute-done.5), channel_id=1, source_target_pairs={{0,1},{1,2},{2,3},{3,4},{4,5},{5,6},{6,7},{7,8},{8,9},{9,10},{10,1... | collective-permute-start | bytes 1572872 | tf_op jit(solution)/shard_map/ppermute | solution.py:70
  236.1 22.0 %collective-permute-start.13 = (bf16[1,16,128,128]{3,2,1,0:T(8,128)(2,1)}, bf16[1,16,128,128]{3,2,1,0:T(8,128)(2,1)}, u32[]{:S(2)}, u32[]{:S(2)}) collective-permute-start(bf16[1,16,128,128]{3,2,1,0:T(8,128)(2,1)} %collective-permute-done.12), channel_id=1, source_target_pairs={{0,15},{1,0},{2,1},{3,2},{4,3},{5,4},{6,5},{7,6},{8,7},{9,8},{10,9... | collective-permute-start | bytes 1572872 | tf_op jit(solution)/shard_map/ppermute | solution.py:72
  248.8 14.7 %collective-permute-start.7 = (bf16[1,16,128,128]{3,2,1,0:T(8,128)(2,1)}, bf16[1,16,128,128]{3,2,1,0:T(8,128)(2,1)}, u32[]{:S(2)}, u32[]{:S(2)}) collective-permute-start(bf16[1,16,128,128]{3,2,1,0:T(8,128)(2,1)} %collective-permute-done.6), channel_id=1, source_target_pairs={{0,1},{1,2},{2,3},{3,4},{4,5},{5,6},{6,7},{7,8},{8,9},{9,10},{10,1... | collective-permute-start | bytes 1572872 | tf_op jit(solution)/shard_map/ppermute | solution.py:70
  258.0 38.4 %copy-start.15 = (bf16[1,16,128,128]{3,2,1,0:T(8,128)(2,1)S(1)}, bf16[1,16,128,128]{3,2,1,0:T(8,128)(2,1)}, u32[]{:S(2)}) copy-start(bf16[1,16,128,128]{3,2,1,0:T(8,128)(2,1)} %copy-done.14) | copy-start | bytes 1572868
  258.0 39.3 %copy-start.13 = (bf16[1,16,128,128]{3,2,1,0:T(8,128)(2,1)S(1)}, bf16[1,16,128,128]{3,2,1,0:T(8,128)(2,1)}, u32[]{:S(2)}) copy-start(bf16[1,16,128,128]{3,2,1,0:T(8,128)(2,1)} %copy-done.12) | copy-start | bytes 1572868
  258.0 40.2 %copy-start.9 = (bf16[1,16,128,128]{3,2,1,0:T(8,128)(2,1)S(1)}, bf16[1,16,128,128]{3,2,1,0:T(8,128)(2,1)}, u32[]{:S(2)}) copy-start(bf16[1,16,128,128]{3,2,1,0:T(8,128)(2,1)} %copy-done.8) | copy-start | bytes 1572868
  258.0 41.0 %copy-start.5 = (bf16[1,16,128,128]{3,2,1,0:T(8,128)(2,1)S(1)}, bf16[1,16,128,128]{3,2,1,0:T(8,128)(2,1)}, u32[]{:S(2)}) copy-start(bf16[1,16,128,128]{3,2,1,0:T(8,128)(2,1)} %copy-done.4) | copy-start | bytes 1572868
  258.0 43.6 %copy-start.3 = (bf16[1,16,128,128]{3,2,1,0:T(8,128)(2,1)S(1)}, bf16[1,16,128,128]{3,2,1,0:T(8,128)(2,1)}, u32[]{:S(2)}) copy-start(bf16[1,16,128,128]{3,2,1,0:T(8,128)(2,1)} %copy-done.2) | copy-start | bytes 1572868
  258.0 44.4 %copy-start.7 = (bf16[1,16,128,128]{3,2,1,0:T(8,128)(2,1)S(1)}, bf16[1,16,128,128]{3,2,1,0:T(8,128)(2,1)}, u32[]{:S(2)}) copy-start(bf16[1,16,128,128]{3,2,1,0:T(8,128)(2,1)} %copy-done.6) | copy-start | bytes 1572868
  258.0 45.2 %copy-start.11 = (bf16[1,16,128,128]{3,2,1,0:T(8,128)(2,1)S(1)}, bf16[1,16,128,128]{3,2,1,0:T(8,128)(2,1)}, u32[]{:S(2)}) copy-start(bf16[1,16,128,128]{3,2,1,0:T(8,128)(2,1)} %copy-done.10) | copy-start | bytes 1572868
  258.1 31.8 %collective-permute-start.14 = (bf16[1,16,128,128]{3,2,1,0:T(8,128)(2,1)}, bf16[1,16,128,128]{3,2,1,0:T(8,128)(2,1)S(1)}, u32[]{:S(2)}, u32[]{:S(2)}) collective-permute-start(bf16[1,16,128,128]{3,2,1,0:T(8,128)(2,1)} %collective-permute-done.13), channel_id=1, source_target_pairs={{0,15},{1,0},{2,1},{3,2},{4,3},{5,4},{6,5},{7,6},{8,7},{9,8},{10,9... | collective-permute-start | bytes 1572872 | tf_op jit(solution)/shard_map/ppermute | solution.py:72
  301.6 27.7 %copy-start = (bf16[64,16,8,128]{3,2,1,0:T(8,128)(2,1)S(1)}, bf16[64,16,8,128]{3,2,1,0:T(8,128)(2,1)}, u32[]{:S(2)}) copy-start(bf16[64,16,8,128]{3,2,1,0:T(8,128)(2,1)} %get-tuple-element.19) | copy-start | bytes 6291460
  301.6 27.7 %copy-start.1 = (f32[16,128,512]{2,1,0:T(8,128)S(1)}, f32[16,128,512]{2,1,0:T(8,128)}, u32[]{:S(2)}) copy-start(f32[16,128,512]{2,1,0:T(8,128)} %fusion.8) | copy-start | bytes 12582916
Sparse Core Ops, SparseCore 0:
  10.4 95.5 all-gather.1
